TPU v7x, 32 devices: a whole 2x2x4 slice. The times are simulated.
32 devices in a mesh: gx: 4 (over z), gy: 2 (over y), gz: 4 (over x, core).
Axes of the slice: x: 2, y: 2, z: 4, core: 2. Of those that a mesh axis runs over, the one named last changes fastest.
Arguments:
- positions: float32 [3, 4, 2, 8, 128], P(None, 'gx', 'gy', 'gz'), may hold values from 0 to 8, as said below
- velocity: float32 [3, 4, 2, 8, 128], P(None, 'gx', 'gy', 'gz'), may hold values from -16 to 16
- counts: int32 [4, 2, 8], P('gx', 'gy', 'gz'), may hold values from 0 to 128, as said below
Outputs:
- velocity_new: float32 [3, 4, 2, 8, 128], P(None, 'gx', 'gy', 'gz')
- pressure: float32 [4, 2, 8, 128], P('gx', 'gy', 'gz')
Inputs may be any that keep to these rules, and one draw needn't show every extreme that they name: `positions`: component k of the position of any slot of tile (a, b, c) lies in [t, t + 1), where t is a, b or c for k = 0, 1, 2. A tile's particles fill its first counts[a, b, c] slots. In every column of tiles the bottom tile is full, the tiles below one topmost wet tile hold 96 or more particles, and the tiles above it are empty.
All inputs are finite; a program needn't handle non-finite values.
Results may differ from a plain program's by a relative error of at most 0.0003.
Values sent between devices are 32-bit elements; how exact they have to be, the bound alone decides.
No kernel may reach another device: no remote copies, remote signals or barrier semaphores. Data moves between devices by JAX's collectives and lax.ppermute only.
A program may use at most 64 MiB of HBM per device.

v0:
```python
import jax
import jax.numpy as jnp
from jax import lax
from jax.sharding import PartitionSpec as P

P_SIZE = 128
ITERS = 3
DIAG_SHIFT = 0.05
VISCOSITY = 0.5
GRAVITY = 0.1
GRADIENT_GAIN = 32.0


def with_halo(cells, sides, width):
    for axis, dim in sides:
        count = lax.axis_size(axis)
        ends = count - 1
        head = lax.slice_in_dim(cells, 0, width, axis=dim)
        tail = lax.slice_in_dim(cells, cells.shape[dim] - width, cells.shape[dim], axis=dim)
        cells = jnp.concatenate(
            [
                lax.ppermute(tail, axis, [(i, (i + 1) % count) for i in range(ends)]),
                cells,
                lax.ppermute(head, axis, [((i + 1) % count, i) for i in range(ends)]),
            ],
            axis=dim,
        )
    return cells


def tile_pairs(rim_positions, rim_valid, rim_field, fold_step, totals):
    size_x = rim_positions.shape[1] - 2
    size_y = rim_positions.shape[2] - 2
    size_z = rim_positions.shape[3] - 2
    slab_tiles = size_y * size_z
    tile_width = rim_positions.shape[4]

    def near_block(source_array, x_start, y_start, z_start):
        zero_start = jnp.zeros((), jnp.int32)
        window = lax.dynamic_slice(
            source_array,
            (zero_start, x_start, y_start, z_start, zero_start),
            (source_array.shape[0], 1, size_y, size_z, tile_width),
        )
        return window.reshape(source_array.shape[0], slab_tiles, tile_width)

    def slab_totals(x_index):
        unit_step = jnp.ones((), jnp.int32)
        own_positions = near_block(rim_positions, x_index + unit_step, unit_step, unit_step)
        own_valid = near_block(rim_valid, x_index + unit_step, unit_step, unit_step)[0]
        start_totals = jax.tree.map(
            lambda item: jnp.zeros((item.shape[0], slab_tiles, item.shape[2]), jnp.float32), totals
        )

        def one_offset(offset_index, carry):
            offset_code = jnp.asarray(offset_index).astype(jnp.int32)
            step_x = offset_code // 9
            step_y = offset_code // 3 % 3
            step_z = offset_code % 3
            near_positions = near_block(rim_positions, x_index + step_x, step_y, step_z)
            near_valid = near_block(rim_valid, x_index + step_x, step_y, step_z)[0]
            near_field = near_block(rim_field, x_index + step_x, step_y, step_z)
            offset = own_positions[:, :, :, None] - near_positions[:, :, None, :]
            distance = offset[0] * offset[0] + offset[1] * offset[1] + offset[2] * offset[2]
            closeness = jnp.maximum(1.0 - distance, 0.0)
            weight = closeness * closeness * own_valid[:, :, None] * near_valid[:, None, :]
            return fold_step(carry, weight, offset, near_field)

        return lax.fori_loop(0, 27, one_offset, start_totals)

    stacked = lax.map(slab_totals, jnp.arange(size_x, dtype=jnp.int32))
    return jax.tree.map(
        lambda block_out: jnp.moveaxis(block_out, 0, 1).reshape(
            block_out.shape[1], size_x * slab_tiles, block_out.shape[3]
        ),
        stacked,
    )


def flat_zeros(rim_positions, components):
    tile_count = (
        (rim_positions.shape[1] - 2) * (rim_positions.shape[2] - 2) * (rim_positions.shape[3] - 2)
    )
    return jnp.zeros((components, tile_count, rim_positions.shape[4]), jnp.float32)


def unflat(flat_values, rim_positions):
    return flat_values.reshape(
        flat_values.shape[0],
        rim_positions.shape[1] - 2,
        rim_positions.shape[2] - 2,
        rim_positions.shape[3] - 2,
        flat_values.shape[2],
    )


def viscous_fold(totals, weight, offset, near_field):
    near_sums, row_sums = totals
    near_sums = near_sums + jnp.einsum(
        "tij,ctj->cti", weight, near_field, precision=lax.Precision.HIGHEST
    )
    return (near_sums, row_sums + jnp.sum(weight, axis=2)[None])


def divergence_fold(totals, weight, offset, near_field):
    lever_sums, flux_sums = totals
    levered = weight[None] * offset
    flux_sums = (
        flux_sums
        + jnp.einsum("ctij,ctj->ti", levered, near_field, precision=lax.Precision.HIGHEST)[None]
    )
    return (lever_sums + jnp.sum(levered, axis=3), flux_sums)


def laplace_fold(totals, weight, offset, near_field):
    return totals + jnp.einsum("tij,ctj->cti", weight, near_field, precision=lax.Precision.HIGHEST)


def gradient_fold(totals, weight, offset, near_field):
    levered = weight[None] * offset
    return totals + jnp.einsum(
        "ctij,tj->cti", levered, near_field[0], precision=lax.Precision.HIGHEST
    )


def viscous_pass(rim_positions, rim_valid, rim_field):
    near_sums, row_sums = tile_pairs(
        rim_positions,
        rim_valid,
        rim_field,
        viscous_fold,
        (flat_zeros(rim_positions, 3), flat_zeros(rim_positions, 1)),
    )
    return (unflat(near_sums, rim_positions), unflat(row_sums, rim_positions))


def divergence_pass(rim_positions, rim_valid, rim_field):
    lever_sums, flux_sums = tile_pairs(
        rim_positions,
        rim_valid,
        rim_field,
        divergence_fold,
        (flat_zeros(rim_positions, 3), flat_zeros(rim_positions, 1)),
    )
    return (unflat(lever_sums, rim_positions), unflat(flux_sums, rim_positions))


def laplace_pass(rim_positions, rim_valid, rim_field):
    return unflat(
        tile_pairs(rim_positions, rim_valid, rim_field, laplace_fold, flat_zeros(rim_positions, 1)),
        rim_positions,
    )


def gradient_pass(rim_positions, rim_valid, rim_field):
    return unflat(
        tile_pairs(
            rim_positions, rim_valid, rim_field, gradient_fold, flat_zeros(rim_positions, 3)
        ),
        rim_positions,
    )


def advance(velocity, valid_mask, near_sums, row_sums):
    gravity_pull = jnp.array([0.0, 0.0, -GRAVITY], jnp.float32).reshape(3, 1, 1, 1, 1)
    return valid_mask * (
        velocity + VISCOSITY / P_SIZE * (near_sums - row_sums * velocity) + gravity_pull
    )


def operate(direction, rim_positions, rim_valid, diagonal):
    rim_direction = with_halo(direction, (("gx", 1), ("gy", 2), ("gz", 3)), 1)
    return (
        rim_direction,
        diagonal * direction - laplace_pass(rim_positions, rim_valid, rim_direction) / P_SIZE,
    )


def paired_sums(residual, precond, applied):
    return lax.psum((jnp.sum(residual * precond), jnp.sum(precond * applied)), ("gx", "gy", "gz"))


def on_device(positions, velocity, counts):
    slot_ids = jnp.arange(positions.shape[4], dtype=jnp.int32)
    valid_mask = (slot_ids[None, None, None, :] < counts[:, :, :, None]).astype(jnp.float32)[None]
    rim_positions, rim_valid, rim_velocity = (
        with_halo(positions, (("gx", 1), ("gy", 2), ("gz", 3)), 1),
        with_halo(valid_mask, (("gx", 1), ("gy", 2), ("gz", 3)), 1),
        with_halo(velocity, (("gx", 1), ("gy", 2), ("gz", 3)), 1),
    )
    near_sums, row_sums = viscous_pass(rim_positions, rim_valid, rim_velocity)
    predicted = advance(velocity, valid_mask, near_sums, row_sums)
    rim_predicted = with_halo(predicted, (("gx", 1), ("gy", 2), ("gz", 3)), 1)
    diagonal = DIAG_SHIFT + row_sums / P_SIZE
    lever_sums, flux_sums = divergence_pass(rim_positions, rim_valid, rim_predicted)
    source = -(GRADIENT_GAIN / P_SIZE) * (
        jnp.sum(predicted * lever_sums, axis=0, keepdims=True) - flux_sums
    )
    pressure = jnp.zeros_like(source)
    residual = source
    precond = residual / diagonal
    rim_search, applied = operate(precond, rim_positions, rim_valid, diagonal)
    norm_now, curvature_sum = paired_sums(residual, precond, applied)
    step_size = norm_now / curvature_sum
    direction = precond
    along = applied
    for iteration in range(ITERS):
        pressure = pressure + step_size * direction
        residual = residual - step_size * along
        if iteration + 1 < ITERS:
            precond = residual / diagonal
            rim_fresh, applied = operate(precond, rim_positions, rim_valid, diagonal)
            norm_next, curvature_sum = paired_sums(residual, precond, applied)
            blend = norm_next / norm_now
            step_size = norm_next / (curvature_sum - blend * norm_next / step_size)
            direction = precond + blend * direction
            along = applied + blend * along
            norm_now = norm_next
    rim_pressure = with_halo(pressure, (("gx", 1), ("gy", 2), ("gz", 3)), 1)
    moments = gradient_pass(rim_positions, rim_valid, rim_pressure)
    velocity_new = predicted - GRADIENT_GAIN / P_SIZE * (pressure * lever_sums - moments)
    return (velocity_new, pressure[0])


def solution(mesh):
    in_specs = (
        P(None, "gx", "gy", "gz", None),
        P(None, "gx", "gy", "gz", None),
        P("gx", "gy", "gz"),
    )
    out_specs = (P(None, "gx", "gy", "gz", None), P("gx", "gy", "gz", None))
    return jax.shard_map(
        on_device, mesh=mesh, in_specs=in_specs, out_specs=out_specs, check_vma=False
    )
```

profile of v0, /device:TPU:1, one launch (start us, length us, event | category | flops | bytes accessed | tf_op | source)
XLA Modules:
  0.0 471.4 jit_solution(9429154291890890409)
XLA Ops:
  1.4 4.1 collective-permute-start.12
  6.8 4.0 collective-permute-start
  10.8 1.3 collective-permute-start.1
  12.1 4.0 collective-permute-start.6
  17.5 3.1 collective-permute-start.14
  22.0 4.0 collective-permute-start.2
  26.0 1.3 collective-permute-start.3
  27.4 5.9 %collective-permute-start.16 = (f32[1,3,3,1,128]{4,3,2,1,0:T(1,128)S(1)}, f32[1,3,3,1,128]{4,3,2,1,0:T(1,128)S(1)}, u32[]{:S(2)}, u32[]{:S(2)}) collective-permute-start(f32[1,3,3,1,128]{4,3,2,1,0:T(1,128)S(1)} %get-tuple-element.1899), channel_id=1, source_target_pairs={{0,1},{1,2},{2,3},{4,5},{5,6},{6,7},{8,9},{9,10},{10,11},{12,13},{... | collective-permute-start | bytes 13832 | tf_op jit(solution)/shard_map/ppermute | solution.py:22
  33.3 1.9 collective-permute-start.17
  35.3 4.3 collective-permute-start.8
  39.6 1.3 collective-permute-start.9
  40.9 3.1 collective-permute-done.9
  44.0 5.1 %collective-permute-start.10 = (f32[3,3,3,1,128]{4,3,2,1,0:T(1,128)S(1)}, f32[3,3,3,1,128]{4,3,2,1,0:T(1,128)S(1)}, u32[]{:S(2)}, u32[]{:S(2)}) collective-permute-start(f32[3,3,3,1,128]{4,3,2,1,0:T(1,128)S(1)} %get-tuple-element.1889), channel_id=1, source_target_pairs={{0,1},{1,2},{2,3},{4,5},{5,6},{6,7},{8,9},{9,10},{10,11},{12,13},{... | collective-permute-start | bytes 41480 | tf_op jit(solution)/shard_map/ppermute | solution.py:22
  49.1 1.9 collective-permute-start.11
  51.1 3.6 collective-permute-start.4
  54.7 1.9 collective-permute-start.5
  56.8 3.0 collective-permute-done.5
  59.8 24.4 %while.152 = (s32[]{:T(128)}, f32[3,2,128]{2,0,1:T(4,128)S(1)}, f32[1,2,128]{2,1,0:T(2,128)S(1)}, f32[3,3,3,4,128]{4,0,3,2,1:T(4,128)S(1)}, f32[3,1,1,2,128]{4,3...) while((s32[]{:T(128)}, f32[3,2,128]{2,0,1:T(4,128)S(1)}, ...), condition=%wide.region_2.3_spmd.clone, body=%wide.region_0.2_spmd.clone.sunk | while | flops 1640740 | bytes 1081868 | solution.py:69
  85.0 4.3 collective-permute-start.18
  90.6 3.0 collective-permute-done.19
  93.6 1.4 collective-permute-start.20
  95.0 1.3 collective-permute-start.21
  96.3 3.1 collective-permute-done.21
  99.4 4.8 %collective-permute-start.22 = (f32[3,3,3,1,128]{4,3,2,1,0:T(1,128)S(1)}, f32[3,3,3,1,128]{4,3,2,1,0:T(1,128)S(1)}, u32[]{:S(2)}, u32[]{:S(2)}) collective-permute-start(f32[3,3,3,1,128]{4,3,2,1,0:T(1,128)S(1)} %get-tuple-element.1887), channel_id=1, source_target_pairs={{0,1},{1,2},{2,3},{4,5},{5,6},{6,7},{8,9},{9,10},{10,11},{12,13},{... | collective-permute-start | bytes 41480 | tf_op jit(solution)/shard_map/ppermute | solution.py:22
  104.2 1.9 collective-permute-start.23
  106.2 3.1 collective-permute-done.23
  109.3 40.3 %while.153 = (s32[]{:T(128)}, f32[3,2,128]{2,1,0:T(2,128)S(1)}, f32[1,2,128]{2,1,0:T(2,128)S(1)}, f32[3,1,1,2,128]{4,3,0,2,1:T(2,128)S(1)}, f32[3,3,3,4,128]{4,3...) while((s32[]{:T(128)}, f32[3,2,128]{2,1,0:T(2,128)S(1)}, ...), condition=%wide.region_5.6_spmd.clone, body=%wide.region_3.5_spmd.clone.sunk | while | flops 2098980 | bytes 1235468 | solution.py:69
  149.6 3.2 collective-permute-start.24
  152.8 1.3 collective-permute-start.25
  154.1 3.0 collective-permute-done.25
  157.1 1.4 collective-permute-start.26
  159.8 3.0 collective-permute-done.27
  162.9 4.8 %collective-permute-start.28 = (f32[1,3,3,1,128]{4,3,2,1,0:T(1,128)S(1)}, f32[1,3,3,1,128]{4,3,2,1,0:T(1,128)S(1)}, u32[]{:S(2)}, u32[]{:S(2)}) collective-permute-start(f32[1,3,3,1,128]{4,3,2,1,0:T(1,128)S(1)} %get-tuple-element.1897), channel_id=1, source_target_pairs={{0,1},{1,2},{2,3},{4,5},{5,6},{6,7},{8,9},{9,10},{10,11},{12,13},{... | collective-permute-start | bytes 13832 | tf_op jit(solution)/shard_map/ppermute | solution.py:22
  167.7 1.9 collective-permute-start.29
  169.6 3.0 collective-permute-done.29
  172.6 21.0 %while.154 = (s32[]{:T(128)}, f32[1,2,128]{2,1,0:T(2,128)S(1)}, f32[1,3,3,4,128]{4,3,2,1,0:T(4,128)S(1)}, f32[3,1,1,2,128]{4,3,2,1,0:T(2,128)S(1)}, f32[3,3,3,4,...) while((s32[]{:T(128)}, f32[1,2,128]{2,1,0:T(2,128)S(1)}, ...), condition=%wide.region_10.11_spmd.clone, body=%wide.region_9.10_spmd.clone.sunk | while | flops 820260 | bytes 811523 | solution.py:69
  194.3 36.9 %all-reduce.2 = (f32[]{:T(128)}, f32[]{:T(128)}) all-reduce(f32[]{:T(128)} %get-tuple-element.1783, f32[]{:T(128)} %get-tuple-element.1782), channel_id=1, replica_groups=mesh['gx'=4,'gy'=2,'gz'=4] {'gx','gy','gz'}, use_global_device_ids=true, to_apply=%region_8.9 | all-reduce | flops 2 | bytes 16 | tf_op jit(solution)/shard_map/psum | solution.py:180
  232.6 2.1 collective-permute-start.30
  235.9 3.0 collective-permute-done.31
  238.9 4.3 collective-permute-start.32
  244.6 3.0 collective-permute-done.33
  247.7 7.3 %collective-permute-start.34 = (f32[1,3,3,1,128]{4,3,2,1,0:T(1,128)S(1)}, f32[1,3,3,1,128]{4,3,2,1,0:T(1,128)S(1)}, u32[]{:S(2)}, u32[]{:S(2)}) collective-permute-start(f32[1,3,3,1,128]{4,3,2,1,0:T(1,128)S(1)} %get-tuple-element.1895), channel_id=1, source_target_pairs={{0,1},{1,2},{2,3},{4,5},{5,6},{6,7},{8,9},{9,10},{10,11},{12,13},{... | collective-permute-start | bytes 13832 | tf_op jit(solution)/shard_map/ppermute | solution.py:22
  255.0 1.9 collective-permute-start.35
  256.9 3.0 collective-permute-done.35
  259.9 21.0 %while.155 = (s32[]{:T(128)}, f32[1,2,128]{2,1,0:T(2,128)S(1)}, f32[1,3,3,4,128]{4,3,2,1,0:T(4,128)S(1)}, f32[3,1,1,2,128]{4,3,2,1,0:T(2,128)S(1)}, f32[3,3,3,4,...) while((s32[]{:T(128)}, f32[1,2,128]{2,1,0:T(2,128)S(1)}, ...), condition=%wide.region_16.17_spmd.clone, body=%wide.region_15.16_spmd.clone.sunk | while | flops 820260 | bytes 811523 | solution.py:69
  281.6 36.1 %all-reduce.1 = (f32[]{:T(128)}, f32[]{:T(128)}) all-reduce(f32[]{:T(128)} %get-tuple-element.1781, f32[]{:T(128)} %get-tuple-element.1780), channel_id=1, replica_groups=mesh['gx'=4,'gy'=2,'gz'=4] {'gx','gy','gz'}, use_global_device_ids=true, to_apply=%region_14.15 | all-reduce | flops 2 | bytes 16 | tf_op jit(solution)/shard_map/psum | solution.py:180
  322.1 2.8 collective-permute-start.36
  326.2 3.0 collective-permute-done.37
  329.2 4.3 collective-permute-start.38
  334.9 3.0 collective-permute-done.39
  337.9 7.3 %collective-permute-start.40 = (f32[1,3,3,1,128]{4,3,2,1,0:T(1,128)S(1)}, f32[1,3,3,1,128]{4,3,2,1,0:T(1,128)S(1)}, u32[]{:S(2)}, u32[]{:S(2)}) collective-permute-start(f32[1,3,3,1,128]{4,3,2,1,0:T(1,128)S(1)} %get-tuple-element.1893), channel_id=1, source_target_pairs={{0,1},{1,2},{2,3},{4,5},{5,6},{6,7},{8,9},{9,10},{10,11},{12,13},{... | collective-permute-start | bytes 13832 | tf_op jit(solution)/shard_map/ppermute | solution.py:22
  345.2 1.9 collective-permute-start.41
  347.2 3.0 collective-permute-done.41
  350.2 21.0 %while.156 = (s32[]{:T(128)}, f32[1,2,128]{2,1,0:T(2,128)S(1)}, f32[1,3,3,4,128]{4,3,2,1,0:T(4,128)S(1)}, f32[3,1,1,2,128]{4,3,2,1,0:T(2,128)S(1)}, f32[3,3,3,4,...) while((s32[]{:T(128)}, f32[1,2,128]{2,1,0:T(2,128)S(1)}, ...), condition=%wide.region_22.23_spmd.clone, body=%wide.region_21.22_spmd.clone.sunk | while | flops 820260 | bytes 811523 | solution.py:69
  371.8 36.1 %all-reduce = (f32[]{:T(128)}, f32[]{:T(128)}) all-reduce(f32[]{:T(128)} %get-tuple-element.1779, f32[]{:T(128)} %get-tuple-element.1778), channel_id=1, replica_groups=mesh['gx'=4,'gy'=2,'gz'=4] {'gx','gy','gz'}, use_global_device_ids=true, to_apply=%region_20.21 | all-reduce | flops 2 | bytes 16 | tf_op jit(solution)/shard_map/psum | solution.py:180
  411.8 2.8 collective-permute-start.42
  414.6 1.3 collective-permute-start.43
  415.9 3.0 collective-permute-done.43
  418.9 4.3 collective-permute-start.44
  425.1 2.4 collective-permute-done.45
  427.6 7.3 %collective-permute-start.46 = (f32[1,3,3,1,128]{4,3,2,1,0:T(1,128)S(1)}, f32[1,3,3,1,128]{4,3,2,1,0:T(1,128)S(1)}, u32[]{:S(2)}, u32[]{:S(2)}) collective-permute-start(f32[1,3,3,1,128]{4,3,2,1,0:T(1,128)S(1)} %get-tuple-element.1891), channel_id=1, source_target_pairs={{0,1},{1,2},{2,3},{4,5},{5,6},{6,7},{8,9},{9,10},{10,11},{12,13},{... | collective-permute-start | bytes 13832 | tf_op jit(solution)/shard_map/ppermute | solution.py:22
  434.9 1.9 collective-permute-start.47
  436.9 3.0 collective-permute-done.47
  439.9 31.0 %while.157 = (s32[]{:T(128)}, f32[3,2,128]{2,1,0:T(2,128)S(1)}, f32[1,3,3,4,128]{4,3,2,1,0:T(4,128)S(1)}, f32[3,1,1,2,128]{4,3,2,1,0:T(2,128)S(1)}, f32[3,3,3,4,...) while((s32[]{:T(128)}, f32[3,2,128]{2,1,0:T(2,128)S(1)}, ...), condition=%wide.region_26.27_spmd.clone, body=%wide.region_25.26_spmd.clone.sunk | while | flops 1804324 | bytes 1088003 | solution.py:69
  (1351 shorter events, 157.0 us)
Async XLA Ops:
  0.6 0.7 copy-start.3
  0.6 6.2 %copy-start.1 = (f32[3,1,1,2,128]{4,3,2,1,0:T(2,128)S(1)}, f32[3,1,1,2,128]{4,3,2,1,0:T(2,128)}, u32[]{:S(2)}) copy-start(f32[3,1,1,2,128]{4,3,2,1,0:T(2,128)} %param.17) | copy-start | bytes 9220
  1.4 10.8 %copy-start = (f32[3,1,1,2,128]{4,3,2,1,0:T(2,128)S(1)}, f32[3,1,1,2,128]{4,3,2,1,0:T(2,128)}, u32[]{:S(2)}) copy-start(f32[3,1,1,2,128]{4,3,2,1,0:T(2,128)} %param.16) | copy-start | bytes 9220
  1.4 14.9 %collective-permute-start.12 = (f32[1,1,1,2,128]{4,3,2,1,0:T(2,128)S(1)}, f32[1,1,1,2,128]{4,3,2,1,0:T(2,128)S(1)}, u32[]{:S(2)}, u32[]{:S(2)}) collective-permute-start(f32[1,1,1,2,128]{4,3,2,1,0:T(2,128)S(1)} %compare_convert_fusion.6), channel_id=1, source_target_pairs={{0,8},{8,16},{16,24},{1,9},{9,17},{17,25},{2,10},{10,18},{18,26},{... | collective-permute-start | bytes 3080 | tf_op jit(solution)/shard_map/ppermute | solution.py:22
  5.5 12.0 %collective-permute-start.13 = (f32[1,1,1,2,128]{4,3,2,1,0:T(2,128)S(1)}, f32[1,1,1,2,128]{4,3,2,1,0:T(2,128)S(1)}, u32[]{:S(2)}, u32[]{:S(2)}) collective-permute-start(f32[1,1,1,2,128]{4,3,2,1,0:T(2,128)S(1)} %compare_convert_fusion.6), channel_id=1, source_target_pairs={{8,0},{16,8},{24,16},{9,1},{17,9},{25,17},{10,2},{18,10},{26,18},{... | collective-permute-start | bytes 3080 | tf_op jit(solution)/shard_map/ppermute | solution.py:24
  6.8 13.8 %collective-permute-start = (f32[3,1,1,2,128]{4,0,3,2,1:T(4,128)S(1)}, f32[3,1,1,2,128]{4,0,3,2,1:T(4,128)S(1)}, u32[]{:S(2)}, u32[]{:S(2)}) collective-permute-start(f32[3,1,1,2,128]{4,0,3,2,1:T(4,128)S(1)} %copy.12), channel_id=1, source_target_pairs={{0,8},{8,16},{16,24},{1,9},{9,17},{17,25},{2,10},{10,18},{18,26},{... | collective-permute-start | bytes 9224 | tf_op jit(solution)/shard_map/ppermute | solution.py:22
  10.8 11.2 %collective-permute-start.1 = (f32[3,1,1,2,128]{4,0,3,2,1:T(4,128)S(1)}, f32[3,1,1,2,128]{4,0,3,2,1:T(4,128)S(1)}, u32[]{:S(2)}, u32[]{:S(2)}) collective-permute-start(f32[3,1,1,2,128]{4,0,3,2,1:T(4,128)S(1)} %copy.12), channel_id=1, source_target_pairs={{8,0},{16,8},{24,16},{9,1},{17,9},{25,17},{10,2},{18,10},{26,18},{... | collective-permute-start | bytes 9224 | tf_op jit(solution)/shard_map/ppermute | solution.py:24
  12.1 13.9 %collective-permute-start.6 = (f32[3,1,1,2,128]{4,3,2,1,0:T(2,128)S(1)}, f32[3,1,1,2,128]{4,3,2,1,0:T(2,128)S(1)}, u32[]{:S(2)}, u32[]{:S(2)}) collective-permute-start(f32[3,1,1,2,128]{4,3,2,1,0:T(2,128)S(1)} %copy-done), channel_id=1, source_target_pairs={{0,8},{8,16},{16,24},{1,9},{9,17},{17,25},{2,10},{10,18},{18,26},{... | collective-permute-start | bytes 9224 | tf_op jit(solution)/shard_map/ppermute | solution.py:22
  16.2 19.1 %collective-permute-start.7 = (f32[3,1,1,2,128]{4,3,2,1,0:T(2,128)S(1)}, f32[3,1,1,2,128]{4,3,2,1,0:T(2,128)S(1)}, u32[]{:S(2)}, u32[]{:S(2)}) collective-permute-start(f32[3,1,1,2,128]{4,3,2,1,0:T(2,128)S(1)} %copy-done), channel_id=1, source_target_pairs={{8,0},{16,8},{24,16},{9,1},{17,9},{25,17},{10,2},{18,10},{26,18},{... | collective-permute-start | bytes 9224 | tf_op jit(solution)/shard_map/ppermute | solution.py:24
  17.5 9.8 %collective-permute-start.14 = (f32[1,3,1,2,128]{4,3,2,1,0:T(2,128)S(1)}, f32[1,3,1,2,128]{4,3,2,1,0:T(2,128)S(1)}, u32[]{:S(2)}, u32[]{:S(2)}) collective-permute-start(f32[1,3,1,2,128]{4,3,2,1,0:T(2,128)S(1)} %pad_maximum_fusion.17), channel_id=1, source_target_pairs={{0,4},{1,5},{2,6},{3,7},{8,12},{9,13},{10,14},{11,15},{16,20},{17,... | collective-permute-start | bytes 9224 | tf_op jit(solution)/shard_map/ppermute | solution.py:22
  20.7 6.7 %collective-permute-start.15 = (f32[1,3,1,2,128]{4,3,2,1,0:T(2,128)S(1)}, f32[1,3,1,2,128]{4,3,2,1,0:T(2,128)S(1)}, u32[]{:S(2)}, u32[]{:S(2)}) collective-permute-start(f32[1,3,1,2,128]{4,3,2,1,0:T(2,128)S(1)} %pad_maximum_fusion.17), channel_id=1, source_target_pairs={{4,0},{5,1},{6,2},{7,3},{12,8},{13,9},{14,10},{15,11},{20,16},{21,... | collective-permute-start | bytes 9224 | tf_op jit(solution)/shard_map/ppermute | solution.py:24
  22.0 29.0 %collective-permute-start.2 = (f32[3,3,1,2,128]{4,0,3,2,1:T(4,128)S(1)}, f32[3,3,1,2,128]{4,0,3,2,1:T(4,128)S(1)}, u32[]{:S(2)}, u32[]{:S(2)}) collective-permute-start(f32[3,3,1,2,128]{4,0,3,2,1:T(4,128)S(1)} %constant_dynamic-update-slice_fusion), channel_id=1, source_target_pairs={{0,4},{1,5},{2,6},{3,7},{8,12},{9,13},{10,14},{11,15},{16,20},{17,... | collective-permute-start | bytes 27656 | tf_op jit(solution)/shard_map/ppermute | solution.py:22
  26.0 25.0 %collective-permute-start.3 = (f32[3,3,1,2,128]{4,0,3,2,1:T(4,128)S(1)}, f32[3,3,1,2,128]{4,0,3,2,1:T(4,128)S(1)}, u32[]{:S(2)}, u32[]{:S(2)}) collective-permute-start(f32[3,3,1,2,128]{4,0,3,2,1:T(4,128)S(1)} %constant_dynamic-update-slice_fusion), channel_id=1, source_target_pairs={{4,0},{5,1},{6,2},{7,3},{12,8},{13,9},{14,10},{15,11},{20,16},{21,... | collective-permute-start | bytes 27656 | tf_op jit(solution)/shard_map/ppermute | solution.py:24
  27.4 12.2 %collective-permute-start.16 = (f32[1,3,3,1,128]{4,3,2,1,0:T(1,128)S(1)}, f32[1,3,3,1,128]{4,3,2,1,0:T(1,128)S(1)}, u32[]{:S(2)}, u32[]{:S(2)}) collective-permute-start(f32[1,3,3,1,128]{4,3,2,1,0:T(1,128)S(1)} %get-tuple-element.1899), channel_id=1, source_target_pairs={{0,1},{1,2},{2,3},{4,5},{5,6},{6,7},{8,9},{9,10},{10,11},{12,13},{... | collective-permute-start | bytes 13832 | tf_op jit(solution)/shard_map/ppermute | solution.py:22
  33.3 7.5 %collective-permute-start.17 = (f32[1,3,3,1,128]{4,3,2,1,0:T(1,128)S(1)}, f32[1,3,3,1,128]{4,3,2,1,0:T(1,128)S(1)}, u32[]{:S(2)}, u32[]{:S(2)}) collective-permute-start(f32[1,3,3,1,128]{4,3,2,1,0:T(1,128)S(1)} %get-tuple-element.1900), channel_id=1, source_target_pairs={{1,0},{2,1},{3,2},{5,4},{6,5},{7,6},{9,8},{10,9},{11,10},{13,12},{... | collective-permute-start | bytes 13832 | tf_op jit(solution)/shard_map/ppermute | solution.py:24
  35.3 5.6 %collective-permute-start.8 = (f32[3,3,1,2,128]{4,3,2,1,0:T(2,128)S(1)}, f32[3,3,1,2,128]{4,3,2,1,0:T(2,128)S(1)}, u32[]{:S(2)}, u32[]{:S(2)}) collective-permute-start(f32[3,3,1,2,128]{4,3,2,1,0:T(2,128)S(1)} %constant_dynamic-update-slice_fusion.3), channel_id=1, source_target_pairs={{0,4},{1,5},{2,6},{3,7},{8,12},{9,13},{10,14},{11,15},{16,20},{17,... | collective-permute-start | bytes 27656 | tf_op jit(solution)/shard_map/ppermute | solution.py:22
  39.6 4.4 collective-permute-start.9
  44.0 12.6 %collective-permute-start.10 = (f32[3,3,3,1,128]{4,3,2,1,0:T(1,128)S(1)}, f32[3,3,3,1,128]{4,3,2,1,0:T(1,128)S(1)}, u32[]{:S(2)}, u32[]{:S(2)}) collective-permute-start(f32[3,3,3,1,128]{4,3,2,1,0:T(1,128)S(1)} %get-tuple-element.1889), channel_id=1, source_target_pairs={{0,1},{1,2},{2,3},{4,5},{5,6},{6,7},{8,9},{9,10},{10,11},{12,13},{... | collective-permute-start | bytes 41480 | tf_op jit(solution)/shard_map/ppermute | solution.py:22
  49.1 7.6 %collective-permute-start.11 = (f32[3,3,3,1,128]{4,3,2,1,0:T(1,128)S(1)}, f32[3,3,3,1,128]{4,3,2,1,0:T(1,128)S(1)}, u32[]{:S(2)}, u32[]{:S(2)}) collective-permute-start(f32[3,3,3,1,128]{4,3,2,1,0:T(1,128)S(1)} %get-tuple-element.1890), channel_id=1, source_target_pairs={{1,0},{2,1},{3,2},{5,4},{6,5},{7,6},{9,8},{10,9},{11,10},{13,12},{... | collective-permute-start | bytes 41480 | tf_op jit(solution)/shard_map/ppermute | solution.py:24
  51.1 5.7 %collective-permute-start.4 = (f32[3,3,3,1,128]{4,0,3,2,1:T(4,128)S(1)}, f32[3,3,3,1,128]{4,0,3,2,1:T(4,128)S(1)}, u32[]{:S(2)}, u32[]{:S(2)}) collective-permute-start(f32[3,3,3,1,128]{4,0,3,2,1:T(4,128)S(1)} %get-tuple-element.1885), channel_id=1, source_target_pairs={{0,1},{1,2},{2,3},{4,5},{5,6},{6,7},{8,9},{9,10},{10,11},{12,13},{... | collective-permute-start | bytes 41480 | tf_op jit(solution)/shard_map/ppermute | solution.py:22
  54.7 5.1 %collective-permute-start.5 = (f32[3,3,3,1,128]{4,0,3,2,1:T(4,128)S(1)}, f32[3,3,3,1,128]{4,0,3,2,1:T(4,128)S(1)}, u32[]{:S(2)}, u32[]{:S(2)}) collective-permute-start(f32[3,3,3,1,128]{4,0,3,2,1:T(4,128)S(1)} %get-tuple-element.1886), channel_id=1, source_target_pairs={{1,0},{2,1},{3,2},{5,4},{6,5},{7,6},{9,8},{10,9},{11,10},{13,12},{... | collective-permute-start | bytes 41480 | tf_op jit(solution)/shard_map/ppermute | solution.py:24
  84.3 0.7 copy-start.2
  85.0 5.6 %collective-permute-start.18 = (f32[3,1,1,2,128]{4,3,2,1,0:T(2,128)S(1)}, f32[3,1,1,2,128]{4,3,2,1,0:T(2,128)S(1)}, u32[]{:S(2)}, u32[]{:S(2)}) collective-permute-start(f32[3,1,1,2,128]{4,3,2,1,0:T(2,128)S(1)} %fusion.106), channel_id=1, source_target_pairs={{0,8},{8,16},{16,24},{1,9},{9,17},{17,25},{2,10},{10,18},{18,26},{... | collective-permute-start | bytes 9224 | tf_op jit(solution)/shard_map/ppermute | solution.py:22
  89.3 4.3 collective-permute-start.19
  93.6 2.7 collective-permute-start.20
  95.0 4.4 collective-permute-start.21
  99.4 6.7 %collective-permute-start.22 = (f32[3,3,3,1,128]{4,3,2,1,0:T(1,128)S(1)}, f32[3,3,3,1,128]{4,3,2,1,0:T(1,128)S(1)}, u32[]{:S(2)}, u32[]{:S(2)}) collective-permute-start(f32[3,3,3,1,128]{4,3,2,1,0:T(1,128)S(1)} %get-tuple-element.1887), channel_id=1, source_target_pairs={{0,1},{1,2},{2,3},{4,5},{5,6},{6,7},{8,9},{9,10},{10,11},{12,13},{... | collective-permute-start | bytes 41480 | tf_op jit(solution)/shard_map/ppermute | solution.py:22
  104.2 5.0 %collective-permute-start.23 = (f32[3,3,3,1,128]{4,3,2,1,0:T(1,128)S(1)}, f32[3,3,3,1,128]{4,3,2,1,0:T(1,128)S(1)}, u32[]{:S(2)}, u32[]{:S(2)}) collective-permute-start(f32[3,3,3,1,128]{4,3,2,1,0:T(1,128)S(1)} %get-tuple-element.1888), channel_id=1, source_target_pairs={{1,0},{2,1},{3,2},{5,4},{6,5},{7,6},{9,8},{10,9},{11,10},{13,12},{... | collective-permute-start | bytes 41480 | tf_op jit(solution)/shard_map/ppermute | solution.py:24
  149.6 4.5 collective-permute-start.24
  152.8 4.3 collective-permute-start.25
  157.1 2.7 collective-permute-start.26
  158.5 4.3 collective-permute-start.27
  162.9 6.7 %collective-permute-start.28 = (f32[1,3,3,1,128]{4,3,2,1,0:T(1,128)S(1)}, f32[1,3,3,1,128]{4,3,2,1,0:T(1,128)S(1)}, u32[]{:S(2)}, u32[]{:S(2)}) collective-permute-start(f32[1,3,3,1,128]{4,3,2,1,0:T(1,128)S(1)} %get-tuple-element.1897), channel_id=1, source_target_pairs={{0,1},{1,2},{2,3},{4,5},{5,6},{6,7},{8,9},{9,10},{10,11},{12,13},{... | collective-permute-start | bytes 13832 | tf_op jit(solution)/shard_map/ppermute | solution.py:22
  167.7 4.9 %collective-permute-start.29 = (f32[1,3,3,1,128]{4,3,2,1,0:T(1,128)S(1)}, f32[1,3,3,1,128]{4,3,2,1,0:T(1,128)S(1)}, u32[]{:S(2)}, u32[]{:S(2)}) collective-permute-start(f32[1,3,3,1,128]{4,3,2,1,0:T(1,128)S(1)} %get-tuple-element.1898), channel_id=1, source_target_pairs={{1,0},{2,1},{3,2},{5,4},{6,5},{7,6},{9,8},{10,9},{11,10},{13,12},{... | collective-permute-start | bytes 13832 | tf_op jit(solution)/shard_map/ppermute | solution.py:24
  232.6 3.4 collective-permute-start.30
  234.6 4.3 collective-permute-start.31
  238.9 5.6 %collective-permute-start.32 = (f32[1,3,1,2,128]{4,3,2,1,0:T(2,128)S(1)}, f32[1,3,1,2,128]{4,3,2,1,0:T(2,128)S(1)}, u32[]{:S(2)}, u32[]{:S(2)}) collective-permute-start(f32[1,3,1,2,128]{4,3,2,1,0:T(2,128)S(1)} %pad_maximum_fusion.19), channel_id=1, source_target_pairs={{0,4},{1,5},{2,6},{3,7},{8,12},{9,13},{10,14},{11,15},{16,20},{17,... | collective-permute-start | bytes 9224 | tf_op jit(solution)/shard_map/ppermute | solution.py:22
  243.3 4.3 collective-permute-start.33
  247.7 9.3 %collective-permute-start.34 = (f32[1,3,3,1,128]{4,3,2,1,0:T(1,128)S(1)}, f32[1,3,3,1,128]{4,3,2,1,0:T(1,128)S(1)}, u32[]{:S(2)}, u32[]{:S(2)}) collective-permute-start(f32[1,3,3,1,128]{4,3,2,1,0:T(1,128)S(1)} %get-tuple-element.1895), channel_id=1, source_target_pairs={{0,1},{1,2},{2,3},{4,5},{5,6},{6,7},{8,9},{9,10},{10,11},{12,13},{... | collective-permute-start | bytes 13832 | tf_op jit(solution)/shard_map/ppermute | solution.py:22
  255.0 4.9 %collective-permute-start.35 = (f32[1,3,3,1,128]{4,3,2,1,0:T(1,128)S(1)}, f32[1,3,3,1,128]{4,3,2,1,0:T(1,128)S(1)}, u32[]{:S(2)}, u32[]{:S(2)}) collective-permute-start(f32[1,3,3,1,128]{4,3,2,1,0:T(1,128)S(1)} %get-tuple-element.1896), channel_id=1, source_target_pairs={{1,0},{2,1},{3,2},{5,4},{6,5},{7,6},{9,8},{10,9},{11,10},{13,12},{... | collective-permute-start | bytes 13832 | tf_op jit(solution)/shard_map/ppermute | solution.py:24
  322.1 4.1 collective-permute-start.36
  324.9 4.3 collective-permute-start.37
  329.2 5.6 %collective-permute-start.38 = (f32[1,3,1,2,128]{4,3,2,1,0:T(2,128)S(1)}, f32[1,3,1,2,128]{4,3,2,1,0:T(2,128)S(1)}, u32[]{:S(2)}, u32[]{:S(2)}) collective-permute-start(f32[1,3,1,2,128]{4,3,2,1,0:T(2,128)S(1)} %pad_maximum_fusion.20), channel_id=1, source_target_pairs={{0,4},{1,5},{2,6},{3,7},{8,12},{9,13},{10,14},{11,15},{16,20},{17,... | collective-permute-start | bytes 9224 | tf_op jit(solution)/shard_map/ppermute | solution.py:22
  333.6 4.3 collective-permute-start.39
  337.9 9.3 %collective-permute-start.40 = (f32[1,3,3,1,128]{4,3,2,1,0:T(1,128)S(1)}, f32[1,3,3,1,128]{4,3,2,1,0:T(1,128)S(1)}, u32[]{:S(2)}, u32[]{:S(2)}) collective-permute-start(f32[1,3,3,1,128]{4,3,2,1,0:T(1,128)S(1)} %get-tuple-element.1893), channel_id=1, source_target_pairs={{0,1},{1,2},{2,3},{4,5},{5,6},{6,7},{8,9},{9,10},{10,11},{12,13},{... | collective-permute-start | bytes 13832 | tf_op jit(solution)/shard_map/ppermute | solution.py:22
  345.2 4.9 %collective-permute-start.41 = (f32[1,3,3,1,128]{4,3,2,1,0:T(1,128)S(1)}, f32[1,3,3,1,128]{4,3,2,1,0:T(1,128)S(1)}, u32[]{:S(2)}, u32[]{:S(2)}) collective-permute-start(f32[1,3,3,1,128]{4,3,2,1,0:T(1,128)S(1)} %get-tuple-element.1894), channel_id=1, source_target_pairs={{1,0},{2,1},{3,2},{5,4},{6,5},{7,6},{9,8},{10,9},{11,10},{13,12},{... | collective-permute-start | bytes 13832 | tf_op jit(solution)/shard_map/ppermute | solution.py:24
  411.8 4.1 collective-permute-start.42
  414.6 4.3 collective-permute-start.43
  418.9 6.2 %collective-permute-start.44 = (f32[1,3,1,2,128]{4,3,2,1,0:T(2,128)S(1)}, f32[1,3,1,2,128]{4,3,2,1,0:T(2,128)S(1)}, u32[]{:S(2)}, u32[]{:S(2)}) collective-permute-start(f32[1,3,1,2,128]{4,3,2,1,0:T(2,128)S(1)} %pad_maximum_fusion.21), channel_id=1, source_target_pairs={{0,4},{1,5},{2,6},{3,7},{8,12},{9,13},{10,14},{11,15},{16,20},{17,... | collective-permute-start | bytes 9224 | tf_op jit(solution)/shard_map/ppermute | solution.py:22
  423.2 4.3 collective-permute-start.45
  427.6 9.3 %collective-permute-start.46 = (f32[1,3,3,1,128]{4,3,2,1,0:T(1,128)S(1)}, f32[1,3,3,1,128]{4,3,2,1,0:T(1,128)S(1)}, u32[]{:S(2)}, u32[]{:S(2)}) collective-permute-start(f32[1,3,3,1,128]{4,3,2,1,0:T(1,128)S(1)} %get-tuple-element.1891), channel_id=1, source_target_pairs={{0,1},{1,2},{2,3},{4,5},{5,6},{6,7},{8,9},{9,10},{10,11},{12,13},{... | collective-permute-start | bytes 13832 | tf_op jit(solution)/shard_map/ppermute | solution.py:22
  434.9 4.9 %collective-permute-start.47 = (f32[1,3,3,1,128]{4,3,2,1,0:T(1,128)S(1)}, f32[1,3,3,1,128]{4,3,2,1,0:T(1,128)S(1)}, u32[]{:S(2)}, u32[]{:S(2)}) collective-permute-start(f32[1,3,3,1,128]{4,3,2,1,0:T(1,128)S(1)} %get-tuple-element.1892), channel_id=1, source_target_pairs={{1,0},{2,1},{3,2},{5,4},{6,5},{7,6},{9,8},{10,9},{11,10},{13,12},{... | collective-permute-start | bytes 13832 | tf_op jit(solution)/shard_map/ppermute | solution.py:24
where the time goes:
time: 473 us; the launch traced here: 471 us
  starting transfers between devices  137 us (29%)
  blocking collectives  109 us (23%)
  matrix products  72 us (15%)
  other arithmetic  63.7 us (13%)
  waiting for transfers between devices  50.9 us (11%)
  loops' own time  19.8 us (4%)
  between operations  11.1 us (2%)
  local copies, waits for them, and re-layouts  8.18 us (2%)
    psum x3, blocking collectives, paired_sums(): lax.psum((jnp.sum(residual * precond), jnp.sum(precond * applied)), ('gx'...  109 us
    ppermute x24, starting transfers between devices, with_halo(): lax.ppermute(tail, axis, [(i, (i + 1) % count) for i in range(ends)])  101 us
    ppermute x24, waiting for transfers between devices, with_halo(): lax.ppermute(head, axis, [((i + 1) % count, i) for i in range(ends)])  50.8 us
    ppermute x24, starting transfers between devices, with_halo(): lax.ppermute(head, axis, [((i + 1) % count, i) for i in range(ends)])  36 us
    dot_general x81, matrix products, laplace_fold(): jnp.einsum('tij,ctj->cti', weight, near_field, precision=lax.Precision.HI...  30.4 us
    sub x162, other arithmetic, one_offset(): offset = own_positions[:, :, :, None] - near_positions[:, :, None, :]  26.4 us
    another operation x6, loops' own time, slab_totals(): return lax.fori_loop(0, 27, one_offset, start_totals)  19.8 us
    dot_general x27, matrix products, divergence_fold(): jnp.einsum('ctij,ctj->ti', levered, near_field, precision=lax.Precision.H...  16.7 us
  transfers between devices with their start and end apart: 48, of which 17 were waited for; matrix products, arithmetic and copies ran while one was open for 0% of the time, Pallas kernels for 0%

commit v1 on v0

--- a/solution.py
+++ b/solution.py
@@ -177,7 +177,9 @@
 
 
 def paired_sums(residual, precond, applied):
-    return lax.psum((jnp.sum(residual * precond), jnp.sum(precond * applied)), ("gx", "gy", "gz"))
+    return lax.psum(
+        lax.psum((jnp.sum(residual * precond), jnp.sum(precond * applied)), ("gy", "gz")), "gx"
+    )
 
 
 def on_device(positions, velocity, counts):

time: 473 us -> 415 us (0.88)
  blocking collectives: 109 us -> 53.4 us
    psum x3 -> x6, blocking collectives: 109 us -> 53.4 us  [the longest x3 30.2 us: paired_sums(): lax.psum((jnp.sum(residual * precond), jnp.sum(precond * applied)), ('gy'...]
where the time goes in v1:
time: 415 us; the launch traced here: 414 us
  starting transfers between devices  134 us (32%)
  matrix products  72 us (17%)
  other arithmetic  63.8 us (15%)
  blocking collectives  53.4 us (13%)
  waiting for transfers between devices  50.9 us (12%)
  loops' own time  19.8 us (5%)
  between operations  11.5 us (3%)
  local copies, waits for them, and re-layouts  8.18 us (2%)
    ppermute x24, starting transfers between devices, with_halo(): lax.ppermute(tail, axis, [(i, (i + 1) % count) for i in range(ends)])  98.2 us
    ppermute x24, waiting for transfers between devices, with_halo(): lax.ppermute(head, axis, [((i + 1) % count, i) for i in range(ends)])  50.8 us
    ppermute x24, starting transfers between devices, with_halo(): lax.ppermute(head, axis, [((i + 1) % count, i) for i in range(ends)])  36 us
    dot_general x81, matrix products, laplace_fold(): jnp.einsum('tij,ctj->cti', weight, near_field, precision=lax.Precision.HI...  30.4 us
    psum x3, blocking collectives, paired_sums(): lax.psum((jnp.sum(residual * precond), jnp.sum(precond * applied)), ('gy'...  30.2 us
    sub x162, other arithmetic, one_offset(): offset = own_positions[:, :, :, None] - near_positions[:, :, None, :]  26.4 us
    psum x3, blocking collectives, paired_sums(): lax.psum(lax.psum((jnp.sum(residual * precond), jnp.sum(precond * applied...  23.1 us
    another operation x6, loops' own time, slab_totals(): return lax.fori_loop(0, 27, one_offset, start_totals)  19.8 us
  transfers between devices with their start and end apart: 48, of which 17 were waited for; matrix products, arithmetic and copies ran while one was open for 0% of the time, Pallas kernels for 0%

profile of v1, /device:TPU:1, one launch (start us, length us, event | category | flops | bytes accessed | tf_op | source)
XLA Modules:
  0.0 413.8 jit_solution(5386418546342816608)
XLA Ops:
  1.4 4.1 %collective-permute-start.12 = (f32[1,1,1,2,128]{4,3,2,1,0:T(2,128)S(1)}, f32[1,1,1,2,128]{4,3,2,1,0:T(2,128)S(1)}, u32[]{:S(2)}, u32[]{:S(2)}) collective-permute-start(f32[1,1,1,2,128]{4,3,2,1,0:T(2,128)S(1)} %compare_convert_fusion.6), channel_id=1, source_target_pairs={{0,8},{8,16},{16,24},{1,9},{9,17},{17,25},{2,10},{10,18},{18,26},{... | collective-permute-start | bytes 3080 | tf_op jit(solution)/shard_map/ppermute | solution.py:22
  6.8 4.0 collective-permute-start
  10.8 1.3 collective-permute-start.1
  12.1 4.0 collective-permute-start.6
  17.5 3.1 collective-permute-start.14
  22.0 4.0 collective-permute-start.2
  26.0 1.3 collective-permute-start.3
  27.4 5.9 %collective-permute-start.16 = (f32[1,3,3,1,128]{4,3,2,1,0:T(1,128)S(1)}, f32[1,3,3,1,128]{4,3,2,1,0:T(1,128)S(1)}, u32[]{:S(2)}, u32[]{:S(2)}) collective-permute-start(f32[1,3,3,1,128]{4,3,2,1,0:T(1,128)S(1)} %get-tuple-element.1905), channel_id=1, source_target_pairs={{0,1},{1,2},{2,3},{4,5},{5,6},{6,7},{8,9},{9,10},{10,11},{12,13},{... | collective-permute-start | bytes 13832 | tf_op jit(solution)/shard_map/ppermute | solution.py:22
  33.3 1.9 collective-permute-start.17
  35.3 4.3 %collective-permute-start.8 = (f32[3,3,1,2,128]{4,3,2,1,0:T(2,128)S(1)}, f32[3,3,1,2,128]{4,3,2,1,0:T(2,128)S(1)}, u32[]{:S(2)}, u32[]{:S(2)}) collective-permute-start(f32[3,3,1,2,128]{4,3,2,1,0:T(2,128)S(1)} %constant_dynamic-update-slice_fusion.3), channel_id=1, source_target_pairs={{0,4},{1,5},{2,6},{3,7},{8,12},{9,13},{10,14},{11,15},{16,20},{17,... | collective-permute-start | bytes 27656 | tf_op jit(solution)/shard_map/ppermute | solution.py:22
  39.6 1.3 collective-permute-start.9
  40.9 3.1 collective-permute-done.9
  44.0 5.1 %collective-permute-start.10 = (f32[3,3,3,1,128]{4,3,2,1,0:T(1,128)S(1)}, f32[3,3,3,1,128]{4,3,2,1,0:T(1,128)S(1)}, u32[]{:S(2)}, u32[]{:S(2)}) collective-permute-start(f32[3,3,3,1,128]{4,3,2,1,0:T(1,128)S(1)} %get-tuple-element.1895), channel_id=1, source_target_pairs={{0,1},{1,2},{2,3},{4,5},{5,6},{6,7},{8,9},{9,10},{10,11},{12,13},{... | collective-permute-start | bytes 41480 | tf_op jit(solution)/shard_map/ppermute | solution.py:22
  49.1 1.9 collective-permute-start.11
  51.1 3.6 collective-permute-start.4
  54.7 1.9 collective-permute-start.5
  56.8 3.0 collective-permute-done.5
  59.8 24.4 %while.152 = (s32[]{:T(128)}, f32[3,2,128]{2,0,1:T(4,128)S(1)}, f32[1,2,128]{2,1,0:T(2,128)S(1)}, f32[3,3,3,4,128]{4,0,3,2,1:T(4,128)S(1)}, f32[3,1,1,2,128]{4,3...) while((s32[]{:T(128)}, f32[3,2,128]{2,0,1:T(4,128)S(1)}, ...), condition=%wide.region_2.3_spmd.clone, body=%wide.region_0.2_spmd.clone.sunk | while | flops 1640740 | bytes 1081868 | solution.py:69
  85.0 4.3 %collective-permute-start.18 = (f32[3,1,1,2,128]{4,3,2,1,0:T(2,128)S(1)}, f32[3,1,1,2,128]{4,3,2,1,0:T(2,128)S(1)}, u32[]{:S(2)}, u32[]{:S(2)}) collective-permute-start(f32[3,1,1,2,128]{4,3,2,1,0:T(2,128)S(1)} %fusion.106), channel_id=1, source_target_pairs={{0,8},{8,16},{16,24},{1,9},{9,17},{17,25},{2,10},{10,18},{18,26},{... | collective-permute-start | bytes 9224 | tf_op jit(solution)/shard_map/ppermute | solution.py:22
  90.6 3.0 collective-permute-done.19
  93.6 1.4 collective-permute-start.20
  96.3 3.1 collective-permute-done.21
  99.4 4.8 %collective-permute-start.22 = (f32[3,3,3,1,128]{4,3,2,1,0:T(1,128)S(1)}, f32[3,3,3,1,128]{4,3,2,1,0:T(1,128)S(1)}, u32[]{:S(2)}, u32[]{:S(2)}) collective-permute-start(f32[3,3,3,1,128]{4,3,2,1,0:T(1,128)S(1)} %get-tuple-element.1893), channel_id=1, source_target_pairs={{0,1},{1,2},{2,3},{4,5},{5,6},{6,7},{8,9},{9,10},{10,11},{12,13},{... | collective-permute-start | bytes 41480 | tf_op jit(solution)/shard_map/ppermute | solution.py:22
  104.2 1.9 collective-permute-start.23
  106.2 3.1 collective-permute-done.23
  109.3 40.3 %while.153 = (s32[]{:T(128)}, f32[3,2,128]{2,1,0:T(2,128)S(1)}, f32[1,2,128]{2,1,0:T(2,128)S(1)}, f32[3,1,1,2,128]{4,3,0,2,1:T(2,128)S(1)}, f32[3,3,3,4,128]{4,3...) while((s32[]{:T(128)}, f32[3,2,128]{2,1,0:T(2,128)S(1)}, ...), condition=%wide.region_5.6_spmd.clone, body=%wide.region_3.5_spmd.clone.sunk | while | flops 2098980 | bytes 1235468 | solution.py:69
  149.6 3.2 collective-permute-start.24
  154.1 3.0 collective-permute-done.25
  157.1 1.4 collective-permute-start.26
  159.8 3.0 collective-permute-done.27
  162.9 4.8 %collective-permute-start.28 = (f32[1,3,3,1,128]{4,3,2,1,0:T(1,128)S(1)}, f32[1,3,3,1,128]{4,3,2,1,0:T(1,128)S(1)}, u32[]{:S(2)}, u32[]{:S(2)}) collective-permute-start(f32[1,3,3,1,128]{4,3,2,1,0:T(1,128)S(1)} %get-tuple-element.1903), channel_id=1, source_target_pairs={{0,1},{1,2},{2,3},{4,5},{5,6},{6,7},{8,9},{9,10},{10,11},{12,13},{... | collective-permute-start | bytes 13832 | tf_op jit(solution)/shard_map/ppermute | solution.py:22
  167.7 1.9 collective-permute-start.29
  169.6 3.0 collective-permute-done.29
  172.6 21.0 %while.154 = (s32[]{:T(128)}, f32[1,2,128]{2,1,0:T(2,128)S(1)}, f32[1,3,3,4,128]{4,3,2,1,0:T(4,128)S(1)}, f32[3,1,1,2,128]{4,3,2,1,0:T(2,128)S(1)}, f32[3,3,3,4,...) while((s32[]{:T(128)}, f32[1,2,128]{2,1,0:T(2,128)S(1)}, ...), condition=%wide.region_11.12_spmd.clone, body=%wide.region_10.11_spmd.clone.sunk | while | flops 820260 | bytes 811523 | solution.py:69
  194.3 10.1 %all-reduce.2 = (f32[]{:T(128)}, f32[]{:T(128)}) all-reduce(f32[]{:T(128)} %get-tuple-element.1783, f32[]{:T(128)} %get-tuple-element.1782), channel_id=1, replica_groups=mesh['gx'=4,'gy'=2,'gz'=4] {'gy','gz'}, use_global_device_ids=true, to_apply=%region_8.9 | all-reduce | flops 2 | bytes 16 | tf_op jit(solution)/shard_map/psum | solution.py:181
  204.3 8.6 %all-reduce.5 = (f32[]{:T(128)}, f32[]{:T(128)}) all-reduce(f32[]{:T(128)} %get-tuple-element.1876, f32[]{:T(128)} %get-tuple-element.1877), channel_id=1, replica_groups=mesh['gx'=4,'gy'=2,'gz'=4] {'gx'}, use_global_device_ids=true, to_apply=%region_9.10 | all-reduce | flops 2 | bytes 16 | tf_op jit(solution)/shard_map/psum | solution.py:180
  214.3 2.0 collective-permute-start.30
  217.7 3.0 collective-permute-done.31
  220.7 2.7 collective-permute-start.32
  224.7 3.0 collective-permute-done.33
  227.7 7.9 %collective-permute-start.34 = (f32[1,3,3,1,128]{4,3,2,1,0:T(1,128)S(1)}, f32[1,3,3,1,128]{4,3,2,1,0:T(1,128)S(1)}, u32[]{:S(2)}, u32[]{:S(2)}) collective-permute-start(f32[1,3,3,1,128]{4,3,2,1,0:T(1,128)S(1)} %get-tuple-element.1901), channel_id=1, source_target_pairs={{0,1},{1,2},{2,3},{4,5},{5,6},{6,7},{8,9},{9,10},{10,11},{12,13},{... | collective-permute-start | bytes 13832 | tf_op jit(solution)/shard_map/ppermute | solution.py:22
  235.6 1.9 collective-permute-start.35
  237.6 3.0 collective-permute-done.35
  240.6 21.0 %while.155 = (s32[]{:T(128)}, f32[1,2,128]{2,1,0:T(2,128)S(1)}, f32[1,3,3,4,128]{4,3,2,1,0:T(4,128)S(1)}, f32[3,1,1,2,128]{4,3,2,1,0:T(2,128)S(1)}, f32[3,3,3,4,...) while((s32[]{:T(128)}, f32[1,2,128]{2,1,0:T(2,128)S(1)}, ...), condition=%wide.region_19.20_spmd.clone, body=%wide.region_18.19_spmd.clone.sunk | while | flops 820260 | bytes 811523 | solution.py:69
  262.3 10.1 %all-reduce.1 = (f32[]{:T(128)}, f32[]{:T(128)}) all-reduce(f32[]{:T(128)} %get-tuple-element.1781, f32[]{:T(128)} %get-tuple-element.1780), channel_id=1, replica_groups=mesh['gx'=4,'gy'=2,'gz'=4] {'gy','gz'}, use_global_device_ids=true, to_apply=%region_16.17 | all-reduce | flops 2 | bytes 16 | tf_op jit(solution)/shard_map/psum | solution.py:181
  272.3 7.3 %all-reduce.4 = (f32[]{:T(128)}, f32[]{:T(128)}) all-reduce(f32[]{:T(128)} %get-tuple-element.1874, f32[]{:T(128)} %get-tuple-element.1875), channel_id=1, replica_groups=mesh['gx'=4,'gy'=2,'gz'=4] {'gx'}, use_global_device_ids=true, to_apply=%region_17.18 | all-reduce | flops 2 | bytes 16 | tf_op jit(solution)/shard_map/psum | solution.py:180
  284.3 3.3 collective-permute-start.36
  288.9 3.0 collective-permute-done.37
  291.9 2.7 collective-permute-start.38
  295.9 3.0 collective-permute-done.39
  299.0 7.9 %collective-permute-start.40 = (f32[1,3,3,1,128]{4,3,2,1,0:T(1,128)S(1)}, f32[1,3,3,1,128]{4,3,2,1,0:T(1,128)S(1)}, u32[]{:S(2)}, u32[]{:S(2)}) collective-permute-start(f32[1,3,3,1,128]{4,3,2,1,0:T(1,128)S(1)} %get-tuple-element.1899), channel_id=1, source_target_pairs={{0,1},{1,2},{2,3},{4,5},{5,6},{6,7},{8,9},{9,10},{10,11},{12,13},{... | collective-permute-start | bytes 13832 | tf_op jit(solution)/shard_map/ppermute | solution.py:22
  306.9 1.9 collective-permute-start.41
  308.8 3.0 collective-permute-done.41
  311.8 21.0 %while.156 = (s32[]{:T(128)}, f32[1,2,128]{2,1,0:T(2,128)S(1)}, f32[1,3,3,4,128]{4,3,2,1,0:T(4,128)S(1)}, f32[3,1,1,2,128]{4,3,2,1,0:T(2,128)S(1)}, f32[3,3,3,4,...) while((s32[]{:T(128)}, f32[1,2,128]{2,1,0:T(2,128)S(1)}, ...), condition=%wide.region_27.28_spmd.clone, body=%wide.region_26.27_spmd.clone.sunk | while | flops 820260 | bytes 811523 | solution.py:69
  333.4 10.1 %all-reduce = (f32[]{:T(128)}, f32[]{:T(128)}) all-reduce(f32[]{:T(128)} %get-tuple-element.1779, f32[]{:T(128)} %get-tuple-element.1778), channel_id=1, replica_groups=mesh['gx'=4,'gy'=2,'gz'=4] {'gy','gz'}, use_global_device_ids=true, to_apply=%region_24.25 | all-reduce | flops 2 | bytes 16 | tf_op jit(solution)/shard_map/psum | solution.py:181
  343.5 7.2 %all-reduce.3 = (f32[]{:T(128)}, f32[]{:T(128)}) all-reduce(f32[]{:T(128)} %get-tuple-element.1872, f32[]{:T(128)} %get-tuple-element.1873), channel_id=1, replica_groups=mesh['gx'=4,'gy'=2,'gz'=4] {'gx'}, use_global_device_ids=true, to_apply=%region_25.26 | all-reduce | flops 2 | bytes 16 | tf_op jit(solution)/shard_map/psum | solution.py:180
  354.7 3.3 collective-permute-start.42
  359.3 3.0 collective-permute-done.43
  362.3 2.7 collective-permute-start.44
  366.9 2.4 collective-permute-done.45
  369.4 7.9 %collective-permute-start.46 = (f32[1,3,3,1,128]{4,3,2,1,0:T(1,128)S(1)}, f32[1,3,3,1,128]{4,3,2,1,0:T(1,128)S(1)}, u32[]{:S(2)}, u32[]{:S(2)}) collective-permute-start(f32[1,3,3,1,128]{4,3,2,1,0:T(1,128)S(1)} %get-tuple-element.1897), channel_id=1, source_target_pairs={{0,1},{1,2},{2,3},{4,5},{5,6},{6,7},{8,9},{9,10},{10,11},{12,13},{... | collective-permute-start | bytes 13832 | tf_op jit(solution)/shard_map/ppermute | solution.py:22
  377.3 1.9 collective-permute-start.47
  379.2 3.0 collective-permute-done.47
  382.2 30.9 %while.157 = (s32[]{:T(128)}, f32[3,2,128]{2,1,0:T(2,128)S(1)}, f32[1,3,3,4,128]{4,3,2,1,0:T(4,128)S(1)}, f32[3,1,1,2,128]{4,3,2,1,0:T(2,128)S(1)}, f32[3,3,3,4,...) while((s32[]{:T(128)}, f32[3,2,128]{2,1,0:T(2,128)S(1)}, ...), condition=%wide.region_32.33_spmd.clone, body=%wide.region_31.32_spmd.clone.sunk | while | flops 1804324 | bytes 1088003 | solution.py:69
  (1354 shorter events, 160.9 us)
Async XLA Ops:
  0.6 0.7 copy-start.3
  0.6 6.2 %copy-start.1 = (f32[3,1,1,2,128]{4,3,2,1,0:T(2,128)S(1)}, f32[3,1,1,2,128]{4,3,2,1,0:T(2,128)}, u32[]{:S(2)}) copy-start(f32[3,1,1,2,128]{4,3,2,1,0:T(2,128)} %param.17) | copy-start | bytes 9220
  1.4 10.8 %copy-start = (f32[3,1,1,2,128]{4,3,2,1,0:T(2,128)S(1)}, f32[3,1,1,2,128]{4,3,2,1,0:T(2,128)}, u32[]{:S(2)}) copy-start(f32[3,1,1,2,128]{4,3,2,1,0:T(2,128)} %param.16) | copy-start | bytes 9220
  1.4 14.9 %collective-permute-start.12 = (f32[1,1,1,2,128]{4,3,2,1,0:T(2,128)S(1)}, f32[1,1,1,2,128]{4,3,2,1,0:T(2,128)S(1)}, u32[]{:S(2)}, u32[]{:S(2)}) collective-permute-start(f32[1,1,1,2,128]{4,3,2,1,0:T(2,128)S(1)} %compare_convert_fusion.6), channel_id=1, source_target_pairs={{0,8},{8,16},{16,24},{1,9},{9,17},{17,25},{2,10},{10,18},{18,26},{... | collective-permute-start | bytes 3080 | tf_op jit(solution)/shard_map/ppermute | solution.py:22
  5.5 12.0 %collective-permute-start.13 = (f32[1,1,1,2,128]{4,3,2,1,0:T(2,128)S(1)}, f32[1,1,1,2,128]{4,3,2,1,0:T(2,128)S(1)}, u32[]{:S(2)}, u32[]{:S(2)}) collective-permute-start(f32[1,1,1,2,128]{4,3,2,1,0:T(2,128)S(1)} %compare_convert_fusion.6), channel_id=1, source_target_pairs={{8,0},{16,8},{24,16},{9,1},{17,9},{25,17},{10,2},{18,10},{26,18},{... | collective-permute-start | bytes 3080 | tf_op jit(solution)/shard_map/ppermute | solution.py:24
  6.8 13.8 %collective-permute-start = (f32[3,1,1,2,128]{4,0,3,2,1:T(4,128)S(1)}, f32[3,1,1,2,128]{4,0,3,2,1:T(4,128)S(1)}, u32[]{:S(2)}, u32[]{:S(2)}) collective-permute-start(f32[3,1,1,2,128]{4,0,3,2,1:T(4,128)S(1)} %copy.12), channel_id=1, source_target_pairs={{0,8},{8,16},{16,24},{1,9},{9,17},{17,25},{2,10},{10,18},{18,26},{... | collective-permute-start | bytes 9224 | tf_op jit(solution)/shard_map/ppermute | solution.py:22
  10.8 11.2 %collective-permute-start.1 = (f32[3,1,1,2,128]{4,0,3,2,1:T(4,128)S(1)}, f32[3,1,1,2,128]{4,0,3,2,1:T(4,128)S(1)}, u32[]{:S(2)}, u32[]{:S(2)}) collective-permute-start(f32[3,1,1,2,128]{4,0,3,2,1:T(4,128)S(1)} %copy.12), channel_id=1, source_target_pairs={{8,0},{16,8},{24,16},{9,1},{17,9},{25,17},{10,2},{18,10},{26,18},{... | collective-permute-start | bytes 9224 | tf_op jit(solution)/shard_map/ppermute | solution.py:24
  12.1 13.9 %collective-permute-start.6 = (f32[3,1,1,2,128]{4,3,2,1,0:T(2,128)S(1)}, f32[3,1,1,2,128]{4,3,2,1,0:T(2,128)S(1)}, u32[]{:S(2)}, u32[]{:S(2)}) collective-permute-start(f32[3,1,1,2,128]{4,3,2,1,0:T(2,128)S(1)} %copy-done), channel_id=1, source_target_pairs={{0,8},{8,16},{16,24},{1,9},{9,17},{17,25},{2,10},{10,18},{18,26},{... | collective-permute-start | bytes 9224 | tf_op jit(solution)/shard_map/ppermute | solution.py:22
  16.2 19.1 %collective-permute-start.7 = (f32[3,1,1,2,128]{4,3,2,1,0:T(2,128)S(1)}, f32[3,1,1,2,128]{4,3,2,1,0:T(2,128)S(1)}, u32[]{:S(2)}, u32[]{:S(2)}) collective-permute-start(f32[3,1,1,2,128]{4,3,2,1,0:T(2,128)S(1)} %copy-done), channel_id=1, source_target_pairs={{8,0},{16,8},{24,16},{9,1},{17,9},{25,17},{10,2},{18,10},{26,18},{... | collective-permute-start | bytes 9224 | tf_op jit(solution)/shard_map/ppermute | solution.py:24
  17.5 9.8 %collective-permute-start.14 = (f32[1,3,1,2,128]{4,3,2,1,0:T(2,128)S(1)}, f32[1,3,1,2,128]{4,3,2,1,0:T(2,128)S(1)}, u32[]{:S(2)}, u32[]{:S(2)}) collective-permute-start(f32[1,3,1,2,128]{4,3,2,1,0:T(2,128)S(1)} %pad_maximum_fusion.17), channel_id=1, source_target_pairs={{0,4},{1,5},{2,6},{3,7},{8,12},{9,13},{10,14},{11,15},{16,20},{17,... | collective-permute-start | bytes 9224 | tf_op jit(solution)/shard_map/ppermute | solution.py:22
  20.7 6.7 %collective-permute-start.15 = (f32[1,3,1,2,128]{4,3,2,1,0:T(2,128)S(1)}, f32[1,3,1,2,128]{4,3,2,1,0:T(2,128)S(1)}, u32[]{:S(2)}, u32[]{:S(2)}) collective-permute-start(f32[1,3,1,2,128]{4,3,2,1,0:T(2,128)S(1)} %pad_maximum_fusion.17), channel_id=1, source_target_pairs={{4,0},{5,1},{6,2},{7,3},{12,8},{13,9},{14,10},{15,11},{20,16},{21,... | collective-permute-start | bytes 9224 | tf_op jit(solution)/shard_map/ppermute | solution.py:24
  22.0 29.0 %collective-permute-start.2 = (f32[3,3,1,2,128]{4,0,3,2,1:T(4,128)S(1)}, f32[3,3,1,2,128]{4,0,3,2,1:T(4,128)S(1)}, u32[]{:S(2)}, u32[]{:S(2)}) collective-permute-start(f32[3,3,1,2,128]{4,0,3,2,1:T(4,128)S(1)} %constant_dynamic-update-slice_fusion), channel_id=1, source_target_pairs={{0,4},{1,5},{2,6},{3,7},{8,12},{9,13},{10,14},{11,15},{16,20},{17,... | collective-permute-start | bytes 27656 | tf_op jit(solution)/shard_map/ppermute | solution.py:22
  26.0 25.0 %collective-permute-start.3 = (f32[3,3,1,2,128]{4,0,3,2,1:T(4,128)S(1)}, f32[3,3,1,2,128]{4,0,3,2,1:T(4,128)S(1)}, u32[]{:S(2)}, u32[]{:S(2)}) collective-permute-start(f32[3,3,1,2,128]{4,0,3,2,1:T(4,128)S(1)} %constant_dynamic-update-slice_fusion), channel_id=1, source_target_pairs={{4,0},{5,1},{6,2},{7,3},{12,8},{13,9},{14,10},{15,11},{20,16},{21,... | collective-permute-start | bytes 27656 | tf_op jit(solution)/shard_map/ppermute | solution.py:24
  27.4 12.2 %collective-permute-start.16 = (f32[1,3,3,1,128]{4,3,2,1,0:T(1,128)S(1)}, f32[1,3,3,1,128]{4,3,2,1,0:T(1,128)S(1)}, u32[]{:S(2)}, u32[]{:S(2)}) collective-permute-start(f32[1,3,3,1,128]{4,3,2,1,0:T(1,128)S(1)} %get-tuple-element.1905), channel_id=1, source_target_pairs={{0,1},{1,2},{2,3},{4,5},{5,6},{6,7},{8,9},{9,10},{10,11},{12,13},{... | collective-permute-start | bytes 13832 | tf_op jit(solution)/shard_map/ppermute | solution.py:22
  33.3 7.5 %collective-permute-start.17 = (f32[1,3,3,1,128]{4,3,2,1,0:T(1,128)S(1)}, f32[1,3,3,1,128]{4,3,2,1,0:T(1,128)S(1)}, u32[]{:S(2)}, u32[]{:S(2)}) collective-permute-start(f32[1,3,3,1,128]{4,3,2,1,0:T(1,128)S(1)} %get-tuple-element.1906), channel_id=1, source_target_pairs={{1,0},{2,1},{3,2},{5,4},{6,5},{7,6},{9,8},{10,9},{11,10},{13,12},{... | collective-permute-start | bytes 13832 | tf_op jit(solution)/shard_map/ppermute | solution.py:24
  35.3 5.6 %collective-permute-start.8 = (f32[3,3,1,2,128]{4,3,2,1,0:T(2,128)S(1)}, f32[3,3,1,2,128]{4,3,2,1,0:T(2,128)S(1)}, u32[]{:S(2)}, u32[]{:S(2)}) collective-permute-start(f32[3,3,1,2,128]{4,3,2,1,0:T(2,128)S(1)} %constant_dynamic-update-slice_fusion.3), channel_id=1, source_target_pairs={{0,4},{1,5},{2,6},{3,7},{8,12},{9,13},{10,14},{11,15},{16,20},{17,... | collective-permute-start | bytes 27656 | tf_op jit(solution)/shard_map/ppermute | solution.py:22
  39.6 4.4 %collective-permute-start.9 = (f32[3,3,1,2,128]{4,3,2,1,0:T(2,128)S(1)}, f32[3,3,1,2,128]{4,3,2,1,0:T(2,128)S(1)}, u32[]{:S(2)}, u32[]{:S(2)}) collective-permute-start(f32[3,3,1,2,128]{4,3,2,1,0:T(2,128)S(1)} %constant_dynamic-update-slice_fusion.3), channel_id=1, source_target_pairs={{4,0},{5,1},{6,2},{7,3},{12,8},{13,9},{14,10},{15,11},{20,16},{21,... | collective-permute-start | bytes 27656 | tf_op jit(solution)/shard_map/ppermute | solution.py:24
  44.0 12.6 %collective-permute-start.10 = (f32[3,3,3,1,128]{4,3,2,1,0:T(1,128)S(1)}, f32[3,3,3,1,128]{4,3,2,1,0:T(1,128)S(1)}, u32[]{:S(2)}, u32[]{:S(2)}) collective-permute-start(f32[3,3,3,1,128]{4,3,2,1,0:T(1,128)S(1)} %get-tuple-element.1895), channel_id=1, source_target_pairs={{0,1},{1,2},{2,3},{4,5},{5,6},{6,7},{8,9},{9,10},{10,11},{12,13},{... | collective-permute-start | bytes 41480 | tf_op jit(solution)/shard_map/ppermute | solution.py:22
  49.1 7.6 %collective-permute-start.11 = (f32[3,3,3,1,128]{4,3,2,1,0:T(1,128)S(1)}, f32[3,3,3,1,128]{4,3,2,1,0:T(1,128)S(1)}, u32[]{:S(2)}, u32[]{:S(2)}) collective-permute-start(f32[3,3,3,1,128]{4,3,2,1,0:T(1,128)S(1)} %get-tuple-element.1896), channel_id=1, source_target_pairs={{1,0},{2,1},{3,2},{5,4},{6,5},{7,6},{9,8},{10,9},{11,10},{13,12},{... | collective-permute-start | bytes 41480 | tf_op jit(solution)/shard_map/ppermute | solution.py:24
  51.1 5.7 %collective-permute-start.4 = (f32[3,3,3,1,128]{4,0,3,2,1:T(4,128)S(1)}, f32[3,3,3,1,128]{4,0,3,2,1:T(4,128)S(1)}, u32[]{:S(2)}, u32[]{:S(2)}) collective-permute-start(f32[3,3,3,1,128]{4,0,3,2,1:T(4,128)S(1)} %get-tuple-element.1891), channel_id=1, source_target_pairs={{0,1},{1,2},{2,3},{4,5},{5,6},{6,7},{8,9},{9,10},{10,11},{12,13},{... | collective-permute-start | bytes 41480 | tf_op jit(solution)/shard_map/ppermute | solution.py:22
  54.7 5.1 %collective-permute-start.5 = (f32[3,3,3,1,128]{4,0,3,2,1:T(4,128)S(1)}, f32[3,3,3,1,128]{4,0,3,2,1:T(4,128)S(1)}, u32[]{:S(2)}, u32[]{:S(2)}) collective-permute-start(f32[3,3,3,1,128]{4,0,3,2,1:T(4,128)S(1)} %get-tuple-element.1892), channel_id=1, source_target_pairs={{1,0},{2,1},{3,2},{5,4},{6,5},{7,6},{9,8},{10,9},{11,10},{13,12},{... | collective-permute-start | bytes 41480 | tf_op jit(solution)/shard_map/ppermute | solution.py:24
  84.3 0.7 copy-start.2
  85.0 5.6 %collective-permute-start.18 = (f32[3,1,1,2,128]{4,3,2,1,0:T(2,128)S(1)}, f32[3,1,1,2,128]{4,3,2,1,0:T(2,128)S(1)}, u32[]{:S(2)}, u32[]{:S(2)}) collective-permute-start(f32[3,1,1,2,128]{4,3,2,1,0:T(2,128)S(1)} %fusion.106), channel_id=1, source_target_pairs={{0,8},{8,16},{16,24},{1,9},{9,17},{17,25},{2,10},{10,18},{18,26},{... | collective-permute-start | bytes 9224 | tf_op jit(solution)/shard_map/ppermute | solution.py:22
  89.3 4.3 %collective-permute-start.19 = (f32[3,1,1,2,128]{4,3,2,1,0:T(2,128)S(1)}, f32[3,1,1,2,128]{4,3,2,1,0:T(2,128)S(1)}, u32[]{:S(2)}, u32[]{:S(2)}) collective-permute-start(f32[3,1,1,2,128]{4,3,2,1,0:T(2,128)S(1)} %fusion.106), channel_id=1, source_target_pairs={{8,0},{16,8},{24,16},{9,1},{17,9},{25,17},{10,2},{18,10},{26,18},{... | collective-permute-start | bytes 9224 | tf_op jit(solution)/shard_map/ppermute | solution.py:24
  93.6 2.7 collective-permute-start.20
  95.0 4.4 %collective-permute-start.21 = (f32[3,3,1,2,128]{4,3,2,1,0:T(2,128)S(1)}, f32[3,3,1,2,128]{4,3,2,1,0:T(2,128)S(1)}, u32[]{:S(2)}, u32[]{:S(2)}) collective-permute-start(f32[3,3,1,2,128]{4,3,2,1,0:T(2,128)S(1)} %pad_maximum_fusion.12), channel_id=1, source_target_pairs={{4,0},{5,1},{6,2},{7,3},{12,8},{13,9},{14,10},{15,11},{20,16},{21,... | collective-permute-start | bytes 27656 | tf_op jit(solution)/shard_map/ppermute | solution.py:24
  99.4 6.7 %collective-permute-start.22 = (f32[3,3,3,1,128]{4,3,2,1,0:T(1,128)S(1)}, f32[3,3,3,1,128]{4,3,2,1,0:T(1,128)S(1)}, u32[]{:S(2)}, u32[]{:S(2)}) collective-permute-start(f32[3,3,3,1,128]{4,3,2,1,0:T(1,128)S(1)} %get-tuple-element.1893), channel_id=1, source_target_pairs={{0,1},{1,2},{2,3},{4,5},{5,6},{6,7},{8,9},{9,10},{10,11},{12,13},{... | collective-permute-start | bytes 41480 | tf_op jit(solution)/shard_map/ppermute | solution.py:22
  104.2 5.0 %collective-permute-start.23 = (f32[3,3,3,1,128]{4,3,2,1,0:T(1,128)S(1)}, f32[3,3,3,1,128]{4,3,2,1,0:T(1,128)S(1)}, u32[]{:S(2)}, u32[]{:S(2)}) collective-permute-start(f32[3,3,3,1,128]{4,3,2,1,0:T(1,128)S(1)} %get-tuple-element.1894), channel_id=1, source_target_pairs={{1,0},{2,1},{3,2},{5,4},{6,5},{7,6},{9,8},{10,9},{11,10},{13,12},{... | collective-permute-start | bytes 41480 | tf_op jit(solution)/shard_map/ppermute | solution.py:24
  149.6 4.5 %collective-permute-start.24 = (f32[1,1,1,2,128]{4,3,2,1,0:T(2,128)S(1)}, f32[1,1,1,2,128]{4,3,2,1,0:T(2,128)S(1)}, u32[]{:S(2)}, u32[]{:S(2)}) collective-permute-start(f32[1,1,1,2,128]{4,3,2,1,0:T(2,128)S(1)} %bitcast_divide_fusion.3), channel_id=1, source_target_pairs={{0,8},{8,16},{16,24},{1,9},{9,17},{17,25},{2,10},{10,18},{18,26},{... | collective-permute-start | bytes 3080 | tf_op jit(solution)/shard_map/ppermute | solution.py:22
  152.8 4.3 %collective-permute-start.25 = (f32[1,1,1,2,128]{4,3,2,1,0:T(2,128)S(1)}, f32[1,1,1,2,128]{4,3,2,1,0:T(2,128)S(1)}, u32[]{:S(2)}, u32[]{:S(2)}) collective-permute-start(f32[1,1,1,2,128]{4,3,2,1,0:T(2,128)S(1)} %bitcast_divide_fusion.3), channel_id=1, source_target_pairs={{8,0},{16,8},{24,16},{9,1},{17,9},{25,17},{10,2},{18,10},{26,18},{... | collective-permute-start | bytes 3080 | tf_op jit(solution)/shard_map/ppermute | solution.py:24
  157.1 2.7 collective-permute-start.26
  158.5 4.3 %collective-permute-start.27 = (f32[1,3,1,2,128]{4,3,2,1,0:T(2,128)S(1)}, f32[1,3,1,2,128]{4,3,2,1,0:T(2,128)S(1)}, u32[]{:S(2)}, u32[]{:S(2)}) collective-permute-start(f32[1,3,1,2,128]{4,3,2,1,0:T(2,128)S(1)} %pad_maximum_fusion.18), channel_id=1, source_target_pairs={{4,0},{5,1},{6,2},{7,3},{12,8},{13,9},{14,10},{15,11},{20,16},{21,... | collective-permute-start | bytes 9224 | tf_op jit(solution)/shard_map/ppermute | solution.py:24
  162.9 6.7 %collective-permute-start.28 = (f32[1,3,3,1,128]{4,3,2,1,0:T(1,128)S(1)}, f32[1,3,3,1,128]{4,3,2,1,0:T(1,128)S(1)}, u32[]{:S(2)}, u32[]{:S(2)}) collective-permute-start(f32[1,3,3,1,128]{4,3,2,1,0:T(1,128)S(1)} %get-tuple-element.1903), channel_id=1, source_target_pairs={{0,1},{1,2},{2,3},{4,5},{5,6},{6,7},{8,9},{9,10},{10,11},{12,13},{... | collective-permute-start | bytes 13832 | tf_op jit(solution)/shard_map/ppermute | solution.py:22
  167.7 4.9 %collective-permute-start.29 = (f32[1,3,3,1,128]{4,3,2,1,0:T(1,128)S(1)}, f32[1,3,3,1,128]{4,3,2,1,0:T(1,128)S(1)}, u32[]{:S(2)}, u32[]{:S(2)}) collective-permute-start(f32[1,3,3,1,128]{4,3,2,1,0:T(1,128)S(1)} %get-tuple-element.1904), channel_id=1, source_target_pairs={{1,0},{2,1},{3,2},{5,4},{6,5},{7,6},{9,8},{10,9},{11,10},{13,12},{... | collective-permute-start | bytes 13832 | tf_op jit(solution)/shard_map/ppermute | solution.py:24
  214.3 3.3 collective-permute-start.30
  216.4 4.3 %collective-permute-start.31 = (f32[1,1,1,2,128]{4,3,2,1,0:T(2,128)S(1)}, f32[1,1,1,2,128]{4,3,2,1,0:T(2,128)S(1)}, u32[]{:S(2)}, u32[]{:S(2)}) collective-permute-start(f32[1,1,1,2,128]{4,3,2,1,0:T(2,128)S(1)} %bitcast_divide_fusion.2), channel_id=1, source_target_pairs={{8,0},{16,8},{24,16},{9,1},{17,9},{25,17},{10,2},{18,10},{26,18},{... | collective-permute-start | bytes 3080 | tf_op jit(solution)/shard_map/ppermute | solution.py:24
  220.7 4.0 collective-permute-start.32
  223.4 4.3 %collective-permute-start.33 = (f32[1,3,1,2,128]{4,3,2,1,0:T(2,128)S(1)}, f32[1,3,1,2,128]{4,3,2,1,0:T(2,128)S(1)}, u32[]{:S(2)}, u32[]{:S(2)}) collective-permute-start(f32[1,3,1,2,128]{4,3,2,1,0:T(2,128)S(1)} %pad_maximum_fusion.19), channel_id=1, source_target_pairs={{4,0},{5,1},{6,2},{7,3},{12,8},{13,9},{14,10},{15,11},{20,16},{21,... | collective-permute-start | bytes 9224 | tf_op jit(solution)/shard_map/ppermute | solution.py:24
  227.7 9.8 %collective-permute-start.34 = (f32[1,3,3,1,128]{4,3,2,1,0:T(1,128)S(1)}, f32[1,3,3,1,128]{4,3,2,1,0:T(1,128)S(1)}, u32[]{:S(2)}, u32[]{:S(2)}) collective-permute-start(f32[1,3,3,1,128]{4,3,2,1,0:T(1,128)S(1)} %get-tuple-element.1901), channel_id=1, source_target_pairs={{0,1},{1,2},{2,3},{4,5},{5,6},{6,7},{8,9},{9,10},{10,11},{12,13},{... | collective-permute-start | bytes 13832 | tf_op jit(solution)/shard_map/ppermute | solution.py:22
  235.6 4.9 %collective-permute-start.35 = (f32[1,3,3,1,128]{4,3,2,1,0:T(1,128)S(1)}, f32[1,3,3,1,128]{4,3,2,1,0:T(1,128)S(1)}, u32[]{:S(2)}, u32[]{:S(2)}) collective-permute-start(f32[1,3,3,1,128]{4,3,2,1,0:T(1,128)S(1)} %get-tuple-element.1902), channel_id=1, source_target_pairs={{1,0},{2,1},{3,2},{5,4},{6,5},{7,6},{9,8},{10,9},{11,10},{13,12},{... | collective-permute-start | bytes 13832 | tf_op jit(solution)/shard_map/ppermute | solution.py:24
  284.3 4.6 %collective-permute-start.36 = (f32[1,1,1,2,128]{4,3,2,1,0:T(2,128)S(1)}, f32[1,1,1,2,128]{4,3,2,1,0:T(2,128)S(1)}, u32[]{:S(2)}, u32[]{:S(2)}) collective-permute-start(f32[1,1,1,2,128]{4,3,2,1,0:T(2,128)S(1)} %fusion.117), channel_id=1, source_target_pairs={{0,8},{8,16},{16,24},{1,9},{9,17},{17,25},{2,10},{10,18},{18,26},{... | collective-permute-start | bytes 3080 | tf_op jit(solution)/shard_map/ppermute | solution.py:22
  287.6 4.3 %collective-permute-start.37 = (f32[1,1,1,2,128]{4,3,2,1,0:T(2,128)S(1)}, f32[1,1,1,2,128]{4,3,2,1,0:T(2,128)S(1)}, u32[]{:S(2)}, u32[]{:S(2)}) collective-permute-start(f32[1,1,1,2,128]{4,3,2,1,0:T(2,128)S(1)} %fusion.117), channel_id=1, source_target_pairs={{8,0},{16,8},{24,16},{9,1},{17,9},{25,17},{10,2},{18,10},{26,18},{... | collective-permute-start | bytes 3080 | tf_op jit(solution)/shard_map/ppermute | solution.py:24
  291.9 4.0 collective-permute-start.38
  294.6 4.3 %collective-permute-start.39 = (f32[1,3,1,2,128]{4,3,2,1,0:T(2,128)S(1)}, f32[1,3,1,2,128]{4,3,2,1,0:T(2,128)S(1)}, u32[]{:S(2)}, u32[]{:S(2)}) collective-permute-start(f32[1,3,1,2,128]{4,3,2,1,0:T(2,128)S(1)} %pad_maximum_fusion.20), channel_id=1, source_target_pairs={{4,0},{5,1},{6,2},{7,3},{12,8},{13,9},{14,10},{15,11},{20,16},{21,... | collective-permute-start | bytes 9224 | tf_op jit(solution)/shard_map/ppermute | solution.py:24
  299.0 9.8 %collective-permute-start.40 = (f32[1,3,3,1,128]{4,3,2,1,0:T(1,128)S(1)}, f32[1,3,3,1,128]{4,3,2,1,0:T(1,128)S(1)}, u32[]{:S(2)}, u32[]{:S(2)}) collective-permute-start(f32[1,3,3,1,128]{4,3,2,1,0:T(1,128)S(1)} %get-tuple-element.1899), channel_id=1, source_target_pairs={{0,1},{1,2},{2,3},{4,5},{5,6},{6,7},{8,9},{9,10},{10,11},{12,13},{... | collective-permute-start | bytes 13832 | tf_op jit(solution)/shard_map/ppermute | solution.py:22
  306.9 4.9 %collective-permute-start.41 = (f32[1,3,3,1,128]{4,3,2,1,0:T(1,128)S(1)}, f32[1,3,3,1,128]{4,3,2,1,0:T(1,128)S(1)}, u32[]{:S(2)}, u32[]{:S(2)}) collective-permute-start(f32[1,3,3,1,128]{4,3,2,1,0:T(1,128)S(1)} %get-tuple-element.1900), channel_id=1, source_target_pairs={{1,0},{2,1},{3,2},{5,4},{6,5},{7,6},{9,8},{10,9},{11,10},{13,12},{... | collective-permute-start | bytes 13832 | tf_op jit(solution)/shard_map/ppermute | solution.py:24
  354.7 4.6 %collective-permute-start.42 = (f32[1,1,1,2,128]{4,3,2,1,0:T(2,128)S(1)}, f32[1,1,1,2,128]{4,3,2,1,0:T(2,128)S(1)}, u32[]{:S(2)}, u32[]{:S(2)}) collective-permute-start(f32[1,1,1,2,128]{4,3,2,1,0:T(2,128)S(1)} %multiply_add_fusion.1), channel_id=1, source_target_pairs={{0,8},{8,16},{16,24},{1,9},{9,17},{17,25},{2,10},{10,18},{18,26},{... | collective-permute-start | bytes 3080 | tf_op jit(solution)/shard_map/ppermute | solution.py:22
  358.0 4.3 %collective-permute-start.43 = (f32[1,1,1,2,128]{4,3,2,1,0:T(2,128)S(1)}, f32[1,1,1,2,128]{4,3,2,1,0:T(2,128)S(1)}, u32[]{:S(2)}, u32[]{:S(2)}) collective-permute-start(f32[1,1,1,2,128]{4,3,2,1,0:T(2,128)S(1)} %multiply_add_fusion.1), channel_id=1, source_target_pairs={{8,0},{16,8},{24,16},{9,1},{17,9},{25,17},{10,2},{18,10},{26,18},{... | collective-permute-start | bytes 3080 | tf_op jit(solution)/shard_map/ppermute | solution.py:24
  362.3 4.6 %collective-permute-start.44 = (f32[1,3,1,2,128]{4,3,2,1,0:T(2,128)S(1)}, f32[1,3,1,2,128]{4,3,2,1,0:T(2,128)S(1)}, u32[]{:S(2)}, u32[]{:S(2)}) collective-permute-start(f32[1,3,1,2,128]{4,3,2,1,0:T(2,128)S(1)} %pad_maximum_fusion.21), channel_id=1, source_target_pairs={{0,4},{1,5},{2,6},{3,7},{8,12},{9,13},{10,14},{11,15},{16,20},{17,... | collective-permute-start | bytes 9224 | tf_op jit(solution)/shard_map/ppermute | solution.py:22
  365.0 4.3 %collective-permute-start.45 = (f32[1,3,1,2,128]{4,3,2,1,0:T(2,128)S(1)}, f32[1,3,1,2,128]{4,3,2,1,0:T(2,128)S(1)}, u32[]{:S(2)}, u32[]{:S(2)}) collective-permute-start(f32[1,3,1,2,128]{4,3,2,1,0:T(2,128)S(1)} %pad_maximum_fusion.21), channel_id=1, source_target_pairs={{4,0},{5,1},{6,2},{7,3},{12,8},{13,9},{14,10},{15,11},{20,16},{21,... | collective-permute-start | bytes 9224 | tf_op jit(solution)/shard_map/ppermute | solution.py:24
  369.4 9.8 %collective-permute-start.46 = (f32[1,3,3,1,128]{4,3,2,1,0:T(1,128)S(1)}, f32[1,3,3,1,128]{4,3,2,1,0:T(1,128)S(1)}, u32[]{:S(2)}, u32[]{:S(2)}) collective-permute-start(f32[1,3,3,1,128]{4,3,2,1,0:T(1,128)S(1)} %get-tuple-element.1897), channel_id=1, source_target_pairs={{0,1},{1,2},{2,3},{4,5},{5,6},{6,7},{8,9},{9,10},{10,11},{12,13},{... | collective-permute-start | bytes 13832 | tf_op jit(solution)/shard_map/ppermute | solution.py:22
  377.3 4.9 %collective-permute-start.47 = (f32[1,3,3,1,128]{4,3,2,1,0:T(1,128)S(1)}, f32[1,3,3,1,128]{4,3,2,1,0:T(1,128)S(1)}, u32[]{:S(2)}, u32[]{:S(2)}) collective-permute-start(f32[1,3,3,1,128]{4,3,2,1,0:T(1,128)S(1)} %get-tuple-element.1898), channel_id=1, source_target_pairs={{1,0},{2,1},{3,2},{5,4},{6,5},{7,6},{9,8},{10,9},{11,10},{13,12},{... | collective-permute-start | bytes 13832 | tf_op jit(solution)/shard_map/ppermute | solution.py:24
